TPU v7x, 512 devices: a whole 4x8x8 slice. The times are simulated.
512 devices in a mesh: area: 128 (over z, y, core), blk: 4 (over x).
Axes of the slice: x: 4, y: 8, z: 8, core: 2. Of those that a mesh axis runs over, the one named last changes fastest.
Arguments:
- activity: float32 [1024, 4, 64, 128], P('area', 'blk'), may hold values from -8 to 8
- ext_input: bfloat16 [1024, 4, 64, 128], P('area', 'blk'), may hold values from -5 to 5
- weights: bfloat16 [384, 4, 128, 512], P('area', 'blk'), may hold values from -0.25 to 0.25
- slot_dst: int32 [384], P('area'), may hold values from 0 to 7
- slot_src: int32 [384], P('area'), may hold values from 0 to 1023, as said below
- slot_count: int32 [128], P('area'), may hold values from 3 to 3, as said below
- hebb_mask: int32 [384], P('area'), may hold values 0 or 1
Outputs:
- final_activity: float32 [1024, 4, 64, 128], P('area', 'blk')
- plasticity: bfloat16 [384, 4, 128, 512], P('area', 'blk')
Inputs may be any that keep to these rules, and one draw needn't show every extreme that they name: Index i of area holds area i // 4; sources lie in areas listed for it by a connectome over the areas that always lists the area itself, the areas beside it on both sides (counted round) and the opposite one. Slots 0, 1 and 2 of index i of area have their source sub-blocks held by indices (i - 1) mod 128, (i + 1) mod 128 and (i + 64) mod 128. Among the occupied slots of one index of area, at most 1 have source sub-blocks held by one index of area (slot_src // 8); some index of area reaches 1. `slot_count`: some index of area has all 3 slots occupied.
All inputs are finite; a program needn't handle non-finite values. No bound on the sum of `hebb_mask` on one device may be relied on, other than what follows from the above.
Results may differ from a plain program's by a relative error of at most 0.014.
Values may be sent and summed in bfloat16 or wider, within the bound.
No kernel may reach another device: no remote copies, remote signals or barrier semaphores. Data moves between devices by JAX's collectives and lax.ppermute only.
A program may use at most 64 MiB of HBM per device.

v0:
```python
import jax
import jax.numpy as jnp
from jax import lax
from jax.sharding import PartitionSpec as P

STEPS = 4
euler_step = 0.5


def request_rosters(src_rows, count_now, sub_dev, n_areas, link_cap):
    slot_cap = src_rows.shape[0]
    slot_ids = jnp.arange(slot_cap)
    occupied = slot_ids < count_now
    owner_idx = src_rows // sub_dev
    local_idx = src_rows % sub_dev
    earlier = (
        (owner_idx[:, None] == owner_idx[None, :])
        & occupied[None, :]
        & (slot_ids[None, :] < slot_ids[:, None])
    )
    link_idx = jnp.minimum(jnp.sum(earlier.astype(jnp.int32), axis=1), link_cap - 1)
    matches = (
        occupied[:, None, None]
        & (owner_idx[:, None, None] == jnp.arange(n_areas)[None, :, None])
        & (link_idx[:, None, None] == jnp.arange(link_cap)[None, None, :])
    )
    request_table = jnp.sum(jnp.where(matches, (local_idx + 1)[:, None, None], 0), axis=0)
    return (occupied, owner_idx, link_idx, request_table)


def body(activity, ext_input, weights, slot_dst, slot_src, slot_count, hebb_mask):
    n_areas = lax.axis_size("area")
    my_blk = lax.axis_index("blk")
    sub_dev = activity.shape[0]
    trials = activity.shape[2]
    quarter = activity.shape[3]
    slot_cap = slot_src.shape[0]
    sub_width = weights.shape[3]
    link_cap = (slot_cap + n_areas - 1) // n_areas
    occupied, owner_idx, link_idx, request_table = request_rosters(
        slot_src, slot_count[0], sub_dev, n_areas, link_cap
    )
    needed_rows = lax.all_to_all(request_table, "area", split_axis=0, concat_axis=0, tiled=True)
    is_valid = needed_rows > 0
    pick_idx = jnp.maximum(needed_rows - 1, 0)
    select = ((slot_dst[:, None] == jnp.arange(sub_dev)[None, :]) & occupied[:, None]).astype(
        jnp.float32
    )
    slot_weights = weights[:, 0]
    pre_list = []
    post_list = []
    full_act, full_ext = (
        lax.all_gather(activity.astype(jnp.bfloat16), "blk", axis=1, tiled=True).astype(
            activity.dtype
        ),
        lax.all_gather(
            ext_input.astype(jnp.float32).astype(jnp.bfloat16), "blk", axis=1, tiled=True
        ).astype(jnp.float32),
    )
    current = full_act.transpose(0, 2, 1, 3).reshape(sub_dev, trials, sub_width)
    drive_in = full_ext.transpose(0, 2, 1, 3).reshape(sub_dev, trials, sub_width)
    rate_full = jnp.tanh(current).astype(jnp.bfloat16)
    for step_idx in range(STEPS):
        rates_own = lax.dynamic_slice_in_dim(rate_full, my_blk * quarter, quarter, 2)
        outbound_rates = jnp.where(
            is_valid[:, :, None, None], rates_own[pick_idx], jnp.zeros((), jnp.bfloat16)
        )
        presynaptic_rates = lax.all_to_all(
            outbound_rates, "area", split_axis=0, concat_axis=0, tiled=True
        )[owner_idx, link_idx]
        input_contribution = jnp.einsum(
            "xvy,xye->xve", presynaptic_rates, slot_weights, preferred_element_type=jnp.float32
        )
        partial_value = jnp.einsum(
            "kd,kts->dts", select, input_contribution, precision=lax.Precision.HIGHEST
        )
        partial_value, presynaptic_rates = (partial_value, presynaptic_rates)
        summed = lax.psum(partial_value.astype(jnp.bfloat16), "blk").astype(jnp.float32)
        current = current + euler_step * (summed - current + drive_in)
        rate_full = jnp.tanh(current).astype(jnp.bfloat16)
        pre_list.append(presynaptic_rates)
        post_list.append(rate_full)
    final_state = lax.dynamic_slice_in_dim(current, my_blk * quarter, quarter, 2)[:, None]
    pre_all = jnp.stack(pre_list, axis=1).astype(jnp.float32)
    pre_centered = (pre_all - jnp.mean(pre_all, axis=2, keepdims=True)).astype(jnp.bfloat16)
    pre_centered = pre_centered.reshape(slot_cap, STEPS * trials, quarter)
    post_all = jnp.stack(post_list, axis=1).astype(jnp.float32)
    post_centered = (post_all - jnp.mean(post_all, axis=2, keepdims=True)).astype(jnp.bfloat16)
    post_slot = post_centered[slot_dst].reshape(slot_cap, STEPS * trials, sub_width)
    change = jnp.einsum("knq,kns->kqs", pre_centered, post_slot, preferred_element_type=jnp.float32)
    gate_on = (occupied & (hebb_mask == 1)).astype(jnp.float32)
    norm_scale = (STEPS * trials) ** (-0.5)
    plasticity = (change * gate_on[:, None, None] * norm_scale).astype(jnp.bfloat16)[:, None]
    return (final_state, plasticity)


def solution(mesh):
    in_specs = (
        P("area", "blk", None, None),
        P("area", "blk", None, None),
        P("area", "blk", None, None),
        P("area"),
        P("area"),
        P("area"),
        P("area"),
    )
    out_specs = (P("area", "blk", None, None), P("area", "blk", None, None))
    return jax.shard_map(body, mesh=mesh, in_specs=in_specs, out_specs=out_specs, check_vma=False)
```

profile of v0, /device:TPU:8, one launch (start us, length us, event | category | flops | bytes accessed | tf_op | source)
XLA Modules:
  0.0 565.2 jit_solution(8893313728588876898)
XLA Ops:
  7.9 0.7 fusion.35
  8.5 1.2 and_convert_fusion
  9.7 0.2 convert_reduce_fusion.2
  9.9 0.6 copy-done.13
  10.5 0.1 fusion.34
  10.6 0.7 copy.91
  11.3 17.4 %all-to-all-start = ((s32[128,1,1]{2,1,0:T(1,128)}), s32[128,1,1]{2,1,0:T(1,128)S(1)}, u32[]{:S(2)}, u32[]{:S(2)}) async-start(s32[128,1,1]{2,1,0:T(1,128)} %copy.91), calls=%async_computation | async-start | bytes 131072 | tf_op jit(solution)/shard_map/all_to_all | solution.py:43
  28.7 1.0 convert_element_type.74
  29.7 13.1 %all_gather.6 = bf16[8,4,64,128]{3,2,1,0:T(8,128)(2,1)S(1)} all-gather(bf16[8,1,64,128]{3,2,1,0:T(8,128)(2,1)S(1)} %convert_element_type.74), channel_id=1, replica_groups=mesh['area'=128,'blk'=4] {'blk'}, dimensions={1}, use_global_device_ids=true | all-gather | bytes 655360 | tf_op jit(solution)/shard_map/all_gather | solution.py:53
  42.8 0.1 convert_bitcast_fusion.1
  43.0 0.6 copy.153
  43.6 0.1 fusion.30
  43.7 2.4 maximum_reduce_fusion
  46.0 2.2 gather_fusion
  48.2 2.4 compare_reduce_fusion
  50.6 3.2 fusion.4
  53.7 13.7 %all-to-all-start.1 = ((bf16[128,1,64,128]{3,2,1,0:T(8,128)(2,1)}), bf16[128,1,64,128]{3,2,1,0:T(8,128)(2,1)S(1)}, u32[]{:S(2)}, u32[]{:S(2)}) async-start(bf16[128,1,64,128]{3,2,1,0:T(8,128)(2,1)} %fusion.4), calls=%async_computation.1 | async-start | bytes 4194304 | tf_op jit(solution)/shard_map/all_to_all | solution.py:68
  67.5 0.7 fusion.42
  68.2 0.7 fusion.32
  68.9 52.5 %all-to-all-done.1 = bf16[128,1,64,128]{3,2,1,0:T(8,128)(2,1)S(1)} async-done(((bf16[128,1,64,128]{3,2,1,0:T(8,128)(2,1)}), bf16[128,1,64,128]{3,2,1,0:T(8,128)(2,1)S(1)}, u32[]{:S(2)}, u32[]{:S(2)}) %all-to-all-start.1) | async-done | bytes 2097184 | tf_op jit(solution)/shard_map/all_to_all | solution.py:68
  121.5 1.2 gather_fusion.1
  122.7 1.0 fusion.28
  123.7 1.7 convolution_convert_fusion.3
  125.5 14.4 %all_gather.7 = bf16[8,4,64,128]{3,2,1,0:T(8,128)(2,1)S(1)} all-gather(bf16[8,1,64,128]{3,2,1,0:T(8,128)(2,1)S(1)} %copy-done.10), channel_id=1, replica_groups=mesh['area'=128,'blk'=4] {'blk'}, dimensions={1}, use_global_device_ids=true | all-gather | bytes 655360 | tf_op jit(solution)/shard_map/all_gather | solution.py:56
  139.8 0.1 convert_bitcast_fusion
  140.0 32.7 %all-reduce.5.cloned.1.call-done = bf16[8,64,512]{2,0,1:T(8,128)(2,1)} async-done(((bf16[8,64,512]{2,0,1:T(8,128)(2,1)}), bf16[8,64,512]{2,0,1:T(8,128)(2,1)}) %all-reduce.5.cloned.1.call-update) | async-done | bytes 524304 | tf_op jit(solution)/shard_map/psum | solution.py:78
  172.6 2.2 tanh_convert_fusion.3
  174.9 0.8 copy-done.4
  175.7 2.2 gather_fusion.2
  177.9 1.8 fusion.3
  179.7 68.1 %all_to_all.29 = bf16[128,1,64,128]{3,2,1,0:T(8,128)(2,1)} all-to-all(bf16[128,1,64,128]{3,2,1,0:T(8,128)(2,1)S(1)} %fusion.3), channel_id=1, replica_groups=mesh['area'=128,'blk'=4] {'area'}, dimensions={0} | all-to-all | bytes 4194304 | tf_op jit(solution)/shard_map/all_to_all | solution.py:68
  247.8 2.2 gather_fusion.3
  250.0 0.2 fusion.26
  250.2 1.7 convolution_convert_fusion.2
  252.0 46.3 %all-reduce.7.cloned.1.call-done = bf16[8,64,512]{2,0,1:T(8,128)(2,1)} async-done(((bf16[8,64,512]{2,0,1:T(8,128)(2,1)}), bf16[8,64,512]{2,0,1:T(8,128)(2,1)}) %all-reduce.7.cloned.1.call-update) | async-done | bytes 524304 | tf_op jit(solution)/shard_map/psum | solution.py:78
  298.3 2.3 tanh_convert_fusion.2
  300.6 0.8 copy-done.2
  301.4 2.2 gather_fusion.4
  303.6 1.8 fusion.2
  305.4 68.1 %all_to_all.30 = bf16[128,1,64,128]{3,2,1,0:T(8,128)(2,1)} all-to-all(bf16[128,1,64,128]{3,2,1,0:T(8,128)(2,1)S(1)} %fusion.2), channel_id=1, replica_groups=mesh['area'=128,'blk'=4] {'area'}, dimensions={0} | all-to-all | bytes 4194304 | tf_op jit(solution)/shard_map/all_to_all | solution.py:68
  373.5 2.2 gather_fusion.5
  375.6 0.2 fusion.24
  375.8 1.7 convolution_convert_fusion.1
  377.5 46.4 %all-reduce.9.cloned.1.call-done = bf16[8,64,512]{2,0,1:T(8,128)(2,1)} async-done(((bf16[8,64,512]{2,0,1:T(8,128)(2,1)}), bf16[8,64,512]{2,0,1:T(8,128)(2,1)}) %all-reduce.9.cloned.1.call-update) | async-done | bytes 524304 | tf_op jit(solution)/shard_map/psum | solution.py:78
  423.9 2.6 tanh_convert_fusion.1
  426.5 0.8 copy-done.6
  427.3 2.1 gather_fusion.6
  429.5 3.1 fusion.1
  432.6 15.0 %all-to-all-start.4 = ((bf16[128,1,64,128]{3,2,1,0:T(8,128)(2,1)}), bf16[128,1,64,128]{3,2,1,0:T(8,128)(2,1)}, u32[]{:S(2)}, u32[]{:S(2)}) async-start(bf16[128,1,64,128]{3,2,1,0:T(8,128)(2,1)} %fusion.1), calls=%async_computation.4 | async-start | bytes 4194304 | tf_op jit(solution)/shard_map/all_to_all | solution.py:68
  447.7 53.6 %all-to-all-done.4 = bf16[128,1,64,128]{3,2,1,0:T(8,128)(2,1)} async-done(((bf16[128,1,64,128]{3,2,1,0:T(8,128)(2,1)}), bf16[128,1,64,128]{3,2,1,0:T(8,128)(2,1)}, u32[]{:S(2)}, u32[]{:S(2)}) %all-to-all-start.4) | async-done | bytes 2097184 | tf_op jit(solution)/shard_map/all_to_all | solution.py:68
  501.2 2.2 gather_fusion.7
  503.4 0.2 fusion.22
  503.6 1.7 convolution_convert_fusion
  505.3 0.1 convert_reduce_fusion.1
  505.4 0.1 fusion.21
  505.4 0.7 copy.106
  506.1 45.5 %all-reduce.11.cloned.1.call-done = bf16[8,64,512]{2,0,1:T(8,128)(2,1)} async-done(((bf16[8,64,512]{2,0,1:T(8,128)(2,1)}), bf16[8,64,512]{2,0,1:T(8,128)(2,1)}) %all-reduce.11.cloned.1.call-update) | async-done | bytes 524304 | tf_op jit(solution)/shard_map/psum | solution.py:78
  551.7 3.0 fusion.16
  554.6 0.3 convert_reduce_fusion
  554.9 0.5 fusion
  555.5 0.7 copy.107
  556.2 0.8 copy.109
  557.0 0.6 gather_fusion.8
  557.6 1.1 fusion.7
  (49 shorter events, 0.5 us)
Async XLA Ops:
  7.2 115.5 %copy-start = (bf16[3,1,128,512]{3,2,1,0:T(8,128)(2,1)S(1)}, bf16[3,1,128,512]{3,2,1,0:T(8,128)(2,1)}, u32[]{:S(2)}) copy-start(bf16[3,1,128,512]{3,2,1,0:T(8,128)(2,1)} %param.9) | copy-start | bytes 1179652
  9.7 19.0 %copy-start.11 = (pred[3]{0:T(512)(128)(4,1)}, pred[3]{0:T(512)(128)(4,1)S(1)}, u32[]{:S(2)}) copy-start(pred[3]{0:T(512)(128)(4,1)S(1)} %get-tuple-element.19) | copy-start | bytes 13
  9.9 0.6 copy-start.13
  11.3 32.3 %all-to-all-start = ((s32[128,1,1]{2,1,0:T(1,128)}), s32[128,1,1]{2,1,0:T(1,128)S(1)}, u32[]{:S(2)}, u32[]{:S(2)}) async-start(s32[128,1,1]{2,1,0:T(1,128)} %copy.91), calls=%async_computation | async-start | bytes 131072 | tf_op jit(solution)/shard_map/all_to_all | solution.py:43
  53.7 67.8 %all-to-all-start.1 = ((bf16[128,1,64,128]{3,2,1,0:T(8,128)(2,1)}), bf16[128,1,64,128]{3,2,1,0:T(8,128)(2,1)S(1)}, u32[]{:S(2)}, u32[]{:S(2)}) async-start(bf16[128,1,64,128]{3,2,1,0:T(8,128)(2,1)} %fusion.4), calls=%async_computation.1 | async-start | bytes 4194304 | tf_op jit(solution)/shard_map/all_to_all | solution.py:68
  67.5 105.2 %all-reduce.5.cloned.1.call-start = ((), (), s32[]{:S(2)}) async-start(), calls=%async_computation.5 | async-start | bytes 1048576 | tf_op jit(solution)/shard_map/psum | solution.py:78
  122.7 2.8 copy-start.10
  125.4 172.9 %all-reduce.7.cloned.1.call-start = ((), (), s32[]{:S(2)}) async-start(), calls=%async_computation.6 | async-start | bytes 1048576 | tf_op jit(solution)/shard_map/psum | solution.py:78
  174.9 0.8 copy-start.4
  247.8 50.5 %copy-start.1 = (bf16[8,64,512]{2,0,1:T(8,128)(2,1)S(1)}, bf16[8,64,512]{2,0,1:T(8,128)(2,1)}, u32[]{:S(2)}) copy-start(bf16[8,64,512]{2,0,1:T(8,128)(2,1)} %all-reduce.5.cloned.1.call-done) | copy-start | bytes 1572868
  251.9 172.0 %all-reduce.9.cloned.1.call-start = ((), (), s32[]{:S(2)}) async-start(), calls=%async_computation.7 | async-start | bytes 1048576 | tf_op jit(solution)/shard_map/psum | solution.py:78
  300.6 0.8 copy-start.2
  426.5 0.8 copy-start.6
  432.6 15.0 %copy-start.14 = (s32[3]{0:T(128)S(1)}, s32[3]{0:T(128)}, u32[]{:S(2)}) copy-start(s32[3]{0:T(128)} %param.10) | copy-start | bytes 40
  432.6 68.6 %all-to-all-start.4 = ((bf16[128,1,64,128]{3,2,1,0:T(8,128)(2,1)}), bf16[128,1,64,128]{3,2,1,0:T(8,128)(2,1)}, u32[]{:S(2)}, u32[]{:S(2)}) async-start(bf16[128,1,64,128]{3,2,1,0:T(8,128)(2,1)} %fusion.1), calls=%async_computation.4 | async-start | bytes 4194304 | tf_op jit(solution)/shard_map/all_to_all | solution.py:68
  447.6 57.7 %copy-start.9 = (bf16[3,64,128]{2,1,0:T(8,128)(2,1)S(1)}, bf16[3,64,128]{2,1,0:T(8,128)(2,1)}, u32[]{:S(2)}) copy-start(bf16[3,64,128]{2,1,0:T(8,128)(2,1)} %gather_fusion.1) | copy-start | bytes 147460
  447.6 104.1 %all-reduce.11.cloned.1.call-start = ((), (), s32[]{:S(2)}) async-start(), calls=%async_computation.8 | async-start | bytes 1048576 | tf_op jit(solution)/shard_map/psum | solution.py:78
  551.7 3.0 copy-start.3
  551.7 3.0 copy-start.5
  551.7 3.0 copy-start.7
  556.2 1.4 copy-start.8
  556.2 1.4 copy-start.12
Sparse Core Ops, SparseCore 0:
  125.5 47.0 all-reduce.4
  252.0 46.2 all-reduce.6
  377.7 46.2 all-reduce.8
  505.4 46.2 all-reduce.10
where the time goes:
time: 566 us; the launch traced here: 565 us
  waiting for transfers between devices  277 us (49%)
  blocking collectives  164 us (29%)
  starting transfers between devices  46.2 us (8%)
  other arithmetic  30.4 us (5%)
  local copies, waits for them, and re-layouts  23.6 us (4%)
  between operations  14.9 us (3%)
  matrix products  9.37 us (2%)
    psum x4, waiting for transfers between devices, body(): lax.psum(partial_value.astype(jnp.bfloat16), 'blk').astype(jnp.float32)  171 us
    all_to_all x2, blocking collectives, body(): lax.all_to_all(outbound_rates, 'area', split_axis=0, concat_axis=0, tiled...  136 us
    all_to_all x2, waiting for transfers between devices, body(): lax.all_to_all(outbound_rates, 'area', split_axis=0, concat_axis=0, tiled...  106 us
    all_to_all x2, starting transfers between devices, body(): lax.all_to_all(outbound_rates, 'area', split_axis=0, concat_axis=0, tiled...  28.7 us
    all_to_all x1, starting transfers between devices, body(): lax.all_to_all(request_table, 'area', split_axis=0, concat_axis=0, tiled=...  17.4 us
    all_gather x1, blocking collectives, body(): lax.all_gather(ext_input.astype(jnp.float32).astype(jnp.bfloat16), 'blk',...  14.4 us
    all_gather x1, blocking collectives, body(): lax.all_gather(activity.astype(jnp.bfloat16), 'blk', axis=1, tiled=True)  13.1 us
  transfers between devices with their start and end apart: 7, of which 6 were waited for; matrix products, arithmetic and copies ran while one was open for 1% of the time, Pallas kernels for 0%

commit v1 on v0

--- a/solution.py
+++ b/solution.py
@@ -1,3 +1,4 @@
+import functools
 import jax
 import jax.numpy as jnp
 from jax import lax
@@ -5,6 +6,13 @@
 
 STEPS = 4
 euler_step = 0.5
+
+
+def shifts_all_finish(sheet, axis_tag):
+    return jnp.sum(lax.all_gather(sheet, axis_tag), 0)
+
+
+resolve_keys = functools.partial(shifts_all_finish, axis_tag="blk")
 
 
 def request_rosters(src_rows, count_now, sub_dev, n_areas, link_cap):
@@ -75,7 +83,7 @@
             "kd,kts->dts", select, input_contribution, precision=lax.Precision.HIGHEST
         )
         partial_value, presynaptic_rates = (partial_value, presynaptic_rates)
-        summed = lax.psum(partial_value.astype(jnp.bfloat16), "blk").astype(jnp.float32)
+        summed = resolve_keys(partial_value.astype(jnp.bfloat16)).astype(jnp.float32)
         current = current + euler_step * (summed - current + drive_in)
         rate_full = jnp.tanh(current).astype(jnp.bfloat16)
         pre_list.append(presynaptic_rates)

time: 566 us -> 495 us (0.87)
  the two profiles are of different devices: /device:TPU:8 before, /device:TPU:1 now
where the time goes in v1:
time: 495 us; the launch traced here: 494 us
  blocking collectives  218 us (44%)
  waiting for transfers between devices  149 us (30%)
  other arithmetic  35.6 us (7%)
  starting transfers between devices  34.4 us (7%)
  local copies, waits for them, and re-layouts  31.6 us (6%)
  between operations  14.9 us (3%)
  matrix products  9.34 us (2%)
    all_to_all x3, blocking collectives, body(): lax.all_to_all(outbound_rates, 'area', split_axis=0, concat_axis=0, tiled...  197 us
    all_gather x4, waiting for transfers between devices, shifts_all_finish(): return jnp.sum(lax.all_gather(sheet, axis_tag), 0)  98.6 us
    all_to_all x1, waiting for transfers between devices, body(): lax.all_to_all(outbound_rates, 'area', split_axis=0, concat_axis=0, tiled...  50.7 us
    all_to_all x1, starting transfers between devices, body(): lax.all_to_all(request_table, 'area', split_axis=0, concat_axis=0, tiled=...  18.4 us
    all_to_all x1, starting transfers between devices, body(): lax.all_to_all(outbound_rates, 'area', split_axis=0, concat_axis=0, tiled...  15.8 us
    all_gather x1, blocking collectives, body(): lax.all_gather(activity.astype(jnp.bfloat16), 'blk', axis=1, tiled=True)  11.7 us
    all_gather x1, blocking collectives, body(): lax.all_gather(ext_input.astype(jnp.float32).astype(jnp.bfloat16), 'blk',...  10 us
  transfers between devices with their start and end apart: 6, of which 5 were waited for; matrix products, arithmetic and copies ran while one was open for 4% of the time, Pallas kernels for 0%

profile of v1, /device:TPU:1, one launch (start us, length us, event | category | flops | bytes accessed | tf_op | source)
XLA Modules:
  0.0 493.7 jit_solution(9332497391056655408)
XLA Ops:
  7.2 0.7 fusion.57
  8.9 0.7 copy.68
  9.6 18.4 %all-to-all-start = ((s32[128,1,1]{2,1,0:T(1,128)}), s32[128,1,1]{2,1,0:T(1,128)S(1)}, u32[]{:S(2)}, u32[]{:S(2)}) async-start(s32[128,1,1]{2,1,0:T(1,128)} %copy.68), calls=%async_computation | async-start | bytes 131072 | tf_op jit(solution)/shard_map/all_to_all | solution.py:51
  28.0 1.0 convert_element_type.188
  29.0 11.7 %all_gather.30 = bf16[8,4,64,128]{3,2,1,0:T(8,128)(2,1)S(1)} all-gather(bf16[8,1,64,128]{3,2,1,0:T(8,128)(2,1)S(1)} %convert_element_type.188), channel_id=1, replica_groups=mesh['area'=128,'blk'=4] {'blk'}, dimensions={1}, use_global_device_ids=true | all-gather | bytes 655360 | tf_op jit(solution)/shard_map/all_gather | solution.py:61
  40.7 1.2 convert_bitcast_fusion.3
  42.1 2.4 maximum_reduce_fusion
  44.5 2.1 gather_fusion
  46.6 2.4 compare_reduce_fusion
  48.9 3.1 fusion.4
  52.1 15.8 %all-to-all-start.1 = ((bf16[128,1,64,128]{3,2,1,0:T(8,128)(2,1)}), bf16[128,1,64,128]{3,2,1,0:T(8,128)(2,1)}, u32[]{:S(2)}, u32[]{:S(2)}) async-start(bf16[128,1,64,128]{3,2,1,0:T(8,128)(2,1)} %fusion.4), calls=%async_computation.1 | async-start | bytes 4194304 | tf_op jit(solution)/shard_map/all_to_all | solution.py:76
  68.0 50.7 %all-to-all-done.1 = bf16[128,1,64,128]{3,2,1,0:T(8,128)(2,1)} async-done(((bf16[128,1,64,128]{3,2,1,0:T(8,128)(2,1)}), bf16[128,1,64,128]{3,2,1,0:T(8,128)(2,1)}, u32[]{:S(2)}, u32[]{:S(2)}) %all-to-all-start.1) | async-done | bytes 2097184 | tf_op jit(solution)/shard_map/all_to_all | solution.py:76
  118.8 2.2 gather_fusion.1
  121.0 0.2 fusion.45
  121.2 1.7 convolution_convert_fusion.3
  123.0 10.0 %all_gather.33 = bf16[8,4,64,128]{3,2,1,0:T(8,128)(2,1)S(1)} all-gather(bf16[8,1,64,128]{3,2,1,0:T(8,128)(2,1)S(1)} %copy-done.19), channel_id=1, replica_groups=mesh['area'=128,'blk'=4] {'blk'}, dimensions={1}, use_global_device_ids=true | all-gather | bytes 655360 | tf_op jit(solution)/shard_map/all_gather | solution.py:64
  133.0 1.2 convert_bitcast_fusion.1
  134.2 20.7 %all-gather.9.cloned.1.call-done = bf16[32,64,512]{2,0,1:T(8,128)(2,1)} async-done(((bf16[8,64,512]{2,0,1:T(8,128)(2,1)}), bf16[32,64,512]{2,0,1:T(8,128)(2,1)}) %all-gather.9.cloned.1.call-update) | async-done | bytes 2097168 | tf_op jit(solution)/shard_map/all_gather | solution.py:12
  154.9 2.0 bitcast_reduce_fusion.3
  156.9 0.3 fusion.10
  157.2 0.5 copy-done.3
  157.8 2.2 gather_fusion.2
  159.9 1.8 fusion.3
  161.8 65.6 %all_to_all.29 = bf16[128,1,64,128]{3,2,1,0:T(8,128)(2,1)} all-to-all(bf16[128,1,64,128]{3,2,1,0:T(8,128)(2,1)S(1)} %fusion.3), channel_id=1, replica_groups=mesh['area'=128,'blk'=4] {'area'}, dimensions={0} | all-to-all | bytes 4194304 | tf_op jit(solution)/shard_map/all_to_all | solution.py:76
  227.4 2.2 gather_fusion.3
  229.7 1.7 convolution_convert_fusion.2
  231.5 30.6 %all-gather.11.cloned.1.call-done = bf16[32,64,512]{2,0,1:T(8,128)(2,1)} async-done(((bf16[8,64,512]{2,0,1:T(8,128)(2,1)}), bf16[32,64,512]{2,0,1:T(8,128)(2,1)}) %all-gather.11.cloned.1.call-update) | async-done | bytes 2097168 | tf_op jit(solution)/shard_map/all_gather | solution.py:12
  262.1 2.0 bitcast_reduce_fusion.2
  264.2 0.8 copy-done.5
  264.9 0.3 fusion.17
  265.2 1.0 copy-done.1
  266.2 2.2 gather_fusion.4
  268.4 1.8 fusion.2
  270.2 65.5 %all_to_all.30 = bf16[128,1,64,128]{3,2,1,0:T(8,128)(2,1)S(1)} all-to-all(bf16[128,1,64,128]{3,2,1,0:T(8,128)(2,1)S(1)} %fusion.2), channel_id=1, replica_groups=mesh['area'=128,'blk'=4] {'area'}, dimensions={0} | all-to-all | bytes 4194304 | tf_op jit(solution)/shard_map/all_to_all | solution.py:76
  335.8 1.2 gather_fusion.5
  336.9 1.0 fusion.41
  337.9 1.7 convolution_convert_fusion.1
  339.7 30.6 %all-gather.13.cloned.1.call-done = bf16[32,64,512]{2,0,1:T(8,128)(2,1)} async-done(((bf16[8,64,512]{2,0,1:T(8,128)(2,1)}), bf16[32,64,512]{2,0,1:T(8,128)(2,1)}) %all-gather.13.cloned.1.call-update) | async-done | bytes 2097168 | tf_op jit(solution)/shard_map/all_gather | solution.py:12
  370.3 2.0 bitcast_reduce_fusion.1
  372.4 0.3 fusion.24
  372.7 1.0 copy-done.10
  373.7 2.2 gather_fusion.6
  375.8 1.8 fusion.1
  377.7 65.6 %all_to_all.31 = bf16[128,1,64,128]{3,2,1,0:T(8,128)(2,1)} all-to-all(bf16[128,1,64,128]{3,2,1,0:T(8,128)(2,1)S(1)} %fusion.1), channel_id=1, replica_groups=mesh['area'=128,'blk'=4] {'area'}, dimensions={0} | all-to-all | bytes 4194304 | tf_op jit(solution)/shard_map/all_to_all | solution.py:76
  443.3 2.2 gather_fusion.7
  445.5 0.2 fusion.39
  445.7 1.7 convolution_convert_fusion
  447.4 1.1 copy.128
  448.5 1.7 copy.72
  450.2 1.6 reshape.454
  451.8 3.0 copy.67
  454.8 2.6 reshape.453
  457.5 3.1 tanh_convert_fusion.1
  460.7 0.7 fusion.38
  461.4 16.7 %all-gather.15.cloned.1.call-done = bf16[32,64,512]{2,0,1:T(8,128)(2,1)} async-done(((bf16[8,64,512]{2,0,1:T(8,128)(2,1)}), bf16[32,64,512]{2,0,1:T(8,128)(2,1)}) %all-gather.15.cloned.1.call-update) | async-done | bytes 2097168 | tf_op jit(solution)/shard_map/all_gather | solution.py:12
  478.2 2.1 bitcast_reduce_fusion
  480.3 1.2 copy_convert_fusion
  481.5 0.6 tanh_convert_fusion
  482.1 0.4 copy-done.7
  482.5 0.4 convert_reduce_fusion
  483.0 0.5 fusion
  483.6 0.6 gather_fusion.8
  484.2 1.9 fusion.49
  486.1 1.1 fusion.7
  (70 shorter events, 1.4 us)
Async XLA Ops:
  7.2 113.8 %copy-start = (bf16[3,1,128,512]{3,2,1,0:T(8,128)(2,1)S(1)}, bf16[3,1,128,512]{3,2,1,0:T(8,128)(2,1)}, u32[]{:S(2)}) copy-start(bf16[3,1,128,512]{3,2,1,0:T(8,128)(2,1)} %param.9) | copy-start | bytes 1179652
  9.6 32.5 %all-to-all-start = ((s32[128,1,1]{2,1,0:T(1,128)}), s32[128,1,1]{2,1,0:T(1,128)S(1)}, u32[]{:S(2)}, u32[]{:S(2)}) async-start(s32[128,1,1]{2,1,0:T(1,128)} %copy.68), calls=%async_computation | async-start | bytes 131072 | tf_op jit(solution)/shard_map/all_to_all | solution.py:51
  52.1 15.9 %copy-start.20 = (s32[3]{0:T(128)S(1)}, s32[3]{0:T(128)}, u32[]{:S(2)}) copy-start(s32[3]{0:T(128)} %param.10) | copy-start | bytes 40
  52.1 66.7 %all-to-all-start.1 = ((bf16[128,1,64,128]{3,2,1,0:T(8,128)(2,1)}), bf16[128,1,64,128]{3,2,1,0:T(8,128)(2,1)}, u32[]{:S(2)}, u32[]{:S(2)}) async-start(bf16[128,1,64,128]{3,2,1,0:T(8,128)(2,1)} %fusion.4), calls=%async_computation.1 | async-start | bytes 4194304 | tf_op jit(solution)/shard_map/all_to_all | solution.py:76
  67.9 55.1 %copy-start.19 = (bf16[8,1,64,128]{3,2,1,0:T(8,128)(2,1)S(1)}, bf16[8,1,64,128]{3,2,1,0:T(8,128)(2,1)}, u32[]{:S(2)}) copy-start(bf16[8,1,64,128]{3,2,1,0:T(8,128)(2,1)} %param.8) | copy-start | bytes 393220
  67.9 87.0 %all-gather.9.cloned.1.call-start = ((), (), s32[]{:S(2)}) async-start(), calls=%async_computation.5 | async-start | bytes 2621440 | tf_op jit(solution)/shard_map/all_gather | solution.py:12
  121.0 2.0 copy-start.12
  122.9 139.2 %all-gather.11.cloned.1.call-start = ((), (), s32[]{:S(2)}) async-start(), calls=%async_computation.6 | async-start | bytes 2621440 | tf_op jit(solution)/shard_map/all_gather | solution.py:12
  156.9 0.8 copy-start.3
  229.5 1.9 copy-start.14
  231.4 138.9 %all-gather.13.cloned.1.call-start = ((), (), s32[]{:S(2)}) async-start(), calls=%async_computation.7 | async-start | bytes 2621440 | tf_op jit(solution)/shard_map/all_gather | solution.py:12
  264.2 0.8 copy-start.5
  265.2 1.0 copy-start.1
  337.9 34.4 %copy-start.2 = (f32[8,64,512]{2,1,0:T(8,128)S(1)}, f32[8,64,512]{2,1,0:T(8,128)}, u32[]{:S(2)}) copy-start(f32[8,64,512]{2,1,0:T(8,128)} %copy-done.1) | copy-start | bytes 3145732
  339.6 138.5 %all-gather.15.cloned.1.call-start = ((), (), s32[]{:S(2)}) async-start(), calls=%async_computation.8 | async-start | bytes 2621440 | tf_op jit(solution)/shard_map/all_gather | solution.py:12
  372.7 1.0 copy-start.10
  445.4 3.0 copy-start.17
  445.5 3.0 copy-start.8
  451.8 5.6 %copy-start.21 = (s32[3]{0:T(128)S(1)}, s32[3]{0:T(128)}, u32[]{:S(2)}) copy-start(s32[3]{0:T(128)} %param.10) | copy-start | bytes 40
  451.8 5.6 %copy-start.22 = (s32[3]{0:T(128)S(1)}, s32[3]{0:T(128)}, u32[]{:S(2)}) copy-start(s32[3]{0:T(128)} %param.13) | copy-start | bytes 40
  451.8 5.7 %copy-start.4 = (bf16[8,64,512]{2,0,1:T(8,128)(2,1)S(1)}, bf16[8,64,512]{2,0,1:T(8,128)(2,1)}, u32[]{:S(2)}) copy-start(bf16[8,64,512]{2,0,1:T(8,128)(2,1)} %copy-done.3) | copy-start | bytes 1572868
  451.8 5.7 %copy-start.6 = (bf16[8,64,512]{2,0,1:T(8,128)(2,1)S(1)}, bf16[8,64,512]{2,0,1:T(8,128)(2,1)}, u32[]{:S(2)}) copy-start(bf16[8,64,512]{2,0,1:T(8,128)(2,1)} %copy-done.5) | copy-start | bytes 1572868
  457.5 3.1 copy-start.13
  457.5 3.1 copy-start.15
  457.5 3.1 copy-start.16
  457.5 3.1 copy-start.18
  478.2 3.3 copy-start.9
  481.5 1.0 copy-start.7
  483.6 2.5 copy-start.11
Sparse Core Ops, SparseCore 0:
  123.0 31.8 all-gather.8
  231.6 30.5 all-gather.10
  339.8 30.5 all-gather.12
  447.5 30.6 all-gather.14
